TPU v7x, 256 devices: a whole 4x4x8 slice. The times are simulated.
256 devices in a mesh: dp: 32 (over x_lo, z, core), tensor: 8 (over x_hi, y).
Axes of the slice: x: 4 (x_hi: 2, x_lo: 2; x = x_hi * 2 + x_lo), y: 4, z: 8, core: 2. Of those that a mesh axis runs over, the one named last changes fastest.
Arguments:
- hidden_input_state: bfloat16 [12288, 4608], P('dp', 'tensor'), may hold values from -80 to 80
- norm_gain: float32 [4608], replicated, may hold values from 0.5 to 1.5
- head_weight: bfloat16 [4608, 8192], P(None, 'tensor'), may hold values from -2 to 2
- target_ids: int32 [12288], P('dp'), may hold values from 0 to 8191
Outputs:
- hidden_state_gradient: float32 [12288, 4608], P('dp', 'tensor')
- grad_head: float32 [4608, 8192], P('dp', 'tensor')
- norm_gain_gradient: float32 [4608], P('tensor')
All inputs are finite; a program needn't handle non-finite values.
Results may differ from a plain program's by a relative error of at most 0.0039.
Values may be sent and summed in bfloat16 or wider, within the bound.
No kernel may reach another device: no remote copies, remote signals or barrier semaphores. Data moves between devices by JAX's collectives and lax.ppermute only.
A program may use at most 192 MiB of HBM per device.

v0:
```python
import jax
import jax.numpy as jnp
from jax import lax
from jax.sharding import PartitionSpec as P

epsilon = 1e-06


def shards(hidden_input_state, norm_gain, head_weight, target_ids):
    local_cols = hidden_input_state.shape[1]
    vocab_rows = head_weight.shape[1]
    width = head_weight.shape[0]
    gathered = lax.all_gather(hidden_input_state, "tensor", axis=1, tiled=True)
    values = gathered.astype(jnp.float32)
    scaled_rows = lax.rsqrt(jnp.mean(values * values, axis=1, keepdims=True) + epsilon)
    normed = (values * scaled_rows * norm_gain[None, :]).astype(jnp.bfloat16)
    logits = jnp.dot(normed, head_weight, preferred_element_type=jnp.float32)
    local_top = jnp.max(logits, axis=1)
    local_total = jnp.sum(jnp.exp(logits - local_top[:, None]), axis=1)
    row_top = lax.pmax(local_top, "tensor")
    row_total = lax.psum(local_total * jnp.exp(local_top - row_top), "tensor")
    log_total = row_top + jnp.log(row_total)
    offset = lax.axis_index("tensor") * vocab_rows
    column_ids = offset + lax.broadcasted_iota(jnp.int32, (1, vocab_rows), 1)
    onehot = (column_ids == target_ids[:, None]).astype(jnp.float32)
    dlogits = (jnp.exp(logits - log_total[:, None]) - onehot).astype(jnp.bfloat16)
    start_col = lax.axis_index("tensor") * local_cols
    normalized_slice = hidden_input_state.astype(jnp.float32) * scaled_rows
    gain_slice = lax.dynamic_slice_in_dim(norm_gain, start_col, local_cols)
    grad_cols = lax.psum_scatter(
        lax.dot_general(
            head_weight, dlogits, (((1,), (1,)), ((), ())), preferred_element_type=jnp.float32
        ),
        "tensor",
        scatter_dimension=0,
        tiled=True,
    )
    normed_gradient = grad_cols.T
    partial_inner_sum = jnp.sum(normed_gradient * gain_slice[None, :] * normalized_slice, axis=1)
    row_inner_sum = lax.psum(partial_inner_sum, "tensor") / width
    weighted_rows = normed_gradient * gain_slice[None, :]
    hidden_state_gradient = scaled_rows * (
        weighted_rows - normalized_slice * row_inner_sum[:, None]
    )
    norm_gain_gradient = lax.psum(jnp.sum(normed_gradient * normalized_slice, axis=0), "dp")
    grad_head = lax.psum_scatter(
        lax.dot_general(
            normed, dlogits, (((0,), (0,)), ((), ())), preferred_element_type=jnp.float32
        ),
        "dp",
        scatter_dimension=0,
        tiled=True,
    )
    return (hidden_state_gradient, grad_head, norm_gain_gradient)


def solution(mesh):
    return jax.shard_map(
        shards,
        mesh=mesh,
        in_specs=(P("dp", "tensor"), P(), P(None, "tensor"), P("dp")),
        out_specs=(P("dp", "tensor"), P("dp", "tensor"), P("tensor")),
        check_vma=False,
    )
```

profile of v0, /device:TPU:4, one launch (start us, length us, event | category | flops | bytes accessed | tf_op | source)
XLA Modules:
  0.0 423.8 jit_solution(17505398155015696289)
XLA Ops:
  7.2 0.0 all-gather.2.cloned.1.call-start
  7.2 0.7 all-gather.2.cloned.1.call-update
  7.9 0.0 reduce-scatter.7.cloned.1.call-start
  8.0 74.1 %all-gather.2.cloned.1.call-done = bf16[384,4608]{0,1:T(8,128)(2,1)} async-done(((bf16[384,576]{0,1:T(8,128)(2,1)}), bf16[384,4608]{0,1:T(8,128)(2,1)}) %all-gather.2.cloned.1.call-update) | async-done | bytes 3538960 | tf_op jit(solution)/shard_map/all_gather | solution.py:13
  82.1 0.0 copy-start
  82.1 3.0 fusion
  85.1 0.1 copy-done
  85.2 8.8 %fusion.8 = (f32[384]{0:T(512)S(1)}, f32[384,1024]{1,0:T(8,128)}) fusion(bf16[4608,1024]{1,0:T(8,128)(2,1)} %param.6, bf16[384,4608]{0,1:T(8,128)(2,1)S(1)} %copy-done, f32[4608]{0:T(1024)} %param.5, f32[384]{0:T(512)S(1)} %add_rsqrt_fusion), kind=kOutput, calls=%fused_computation.21 | convolution fusion | flops 3631349248 | bytes 14570496 | tf_op jit(solution)/shard_map/dot_general | solution.py:17
  93.9 22.2 %pmax.7 = f32[384]{0:T(512)S(1)} all-reduce(f32[384]{0:T(512)S(1)} %get-tuple-element.11), channel_id=1, replica_groups=mesh['dp'=32,'tensor'=8] {'tensor'}, use_global_device_ids=true, to_apply=%region_2.0 | all-reduce | flops 384 | bytes 3072 | tf_op jit(solution)/shard_map/pmax | solution.py:20
  116.1 1.8 exponential_reduce_fusion
  117.9 0.6 exponential_multiply_fusion
  118.5 19.1 %psum.21 = f32[384]{0:T(512)S(1)} all-reduce(f32[384]{0:T(512)} %exponential_multiply_fusion), channel_id=1, replica_groups=mesh['dp'=32,'tensor'=8] {'tensor'}, use_global_device_ids=true, to_apply=%region_4.0 | all-reduce | flops 384 | bytes 3072 | tf_op jit(solution)/shard_map/psum | solution.py:21
  137.6 0.0 copy-start.2
  137.6 0.6 copy-done.2
  138.2 11.1 %convolution_bitcast_fusion = f32[4608,384]{0,1:T(8,128)} fusion(bf16[4608,1024]{1,0:T(8,128)(2,1)} %param.6, f32[384,1024]{1,0:T(8,128)} %get-tuple-element.12, s32[1024]{0:T(1024)S(1)} %iota_add_fusion, f32[384]{0:T(512)S(1)} %log_add_fusion, s32[384]{0:T(512)} %param.7), kind=kOutput, calls=%fused_computation.2 | convolution fusion | flops 3625844736 | bytes 18095104 | tf_op jit(solution)/shard_map/dot_general | solution.py:31
  149.2 8.0 %copy.11 = f32[4608,384]{1,0:T(8,128)} copy(f32[4608,384]{0,1:T(8,128)} %convolution_bitcast_fusion) | data formatting | bytes 14155776
  157.3 0.0 copy-start.3
  157.3 0.0 copy-start.4
  157.3 0.0 reduce-scatter.7.cloned.1.call-update
  157.3 0.2 reduce-scatter.5.cloned.1.call-start
  157.5 0.4 copy-done.3
  158.0 0.0 copy-done.4
  158.0 11.5 %fusion.3 = f32[4608,1024]{1,0:T(8,128)} fusion(bf16[384,4608]{0,1:T(8,128)(2,1)S(1)} %copy-done, f32[4608]{0:T(1024)} %param.5, f32[384]{0:T(512)S(1)} %add_rsqrt_fusion, f32[384,1024]{1,0:T(8,128)} %get-tuple-element.12, s32[1024]{0:T(1024)S(1)} %iota_add_fusion, f32[384]{0:T(512)S(1)} %copy-done.3, s32[384]{0:T(512)S(1)} %copy-done.4), kind=kOutput, calls=%fused_computation.8 | convolution fusion | flops 3632922624 | bytes 24013312 | tf_op jit(solution)/shard_map/dot_general | solution.py:47
  169.5 0.0 copy-start.1
  169.5 0.0 reduce-scatter.5.cloned.1.call-update
  169.5 1.1 copy-done.1
  170.6 0.3 copy.9
  170.9 0.8 dynamic_slice.3
  171.6 93.7 %reduce-scatter.7.cloned.1.call-done = f32[576,384]{1,0:T(8,128)} async-done(((f32[4608,384]{1,0:T(8,128)}), f32[576,384]{1,0:T(8,128)}) %reduce-scatter.7.cloned.1.call-update) | async-done | bytes 884752
  265.3 1.5 copy.12
  266.8 0.4 fusion.7
  267.3 23.4 %psum.22 = f32[384]{0:T(512)S(1)} all-reduce(f32[384]{0:T(512)S(1)} %get-tuple-element.10), channel_id=1, replica_groups=mesh['dp'=32,'tensor'=8] {'tensor'}, use_global_device_ids=true, to_apply=%region_7.0 | all-reduce | flops 384 | bytes 3072 | tf_op jit(solution)/shard_map/psum | solution.py:40
  290.7 0.2 subtract_multiply_fusion
  290.9 1.2 copy.10
  292.2 54.0 %psum.23 = f32[576]{0:T(1024)} all-reduce(f32[576]{0:T(1024)S(1)} %get-tuple-element.9), channel_id=1, replica_groups=mesh['dp'=32,'tensor'=8] {'dp'}, use_global_device_ids=true, to_apply=%region_10.0 | all-reduce | flops 576 | bytes 4608 | tf_op jit(solution)/shard_map/psum | solution.py:45
  346.2 71.0 %reduce-scatter.5.cloned.1.call-done = f32[144,1024]{1,0:T(8,128)} async-done(((f32[4608,1024]{1,0:T(8,128)}), f32[144,1024]{1,0:T(8,128)}) %reduce-scatter.5.cloned.1.call-update) | async-done | bytes 589840 | tf_op jit(solution)/shard_map/reduce_scatter | solution.py:46
  (4 shorter events, 0.0 us)
Async XLA Ops:
  7.2 74.9 %all-gather.2.cloned.1.call-start = ((), (), s32[]{:S(2)}) async-start(), calls=%async_computation.2 | async-start | bytes 3981312 | tf_op jit(solution)/shard_map/all_gather | solution.py:13
  7.9 257.4 %reduce-scatter.7.cloned.1.call-start = ((), (), s32[]{:S(2)}) async-start(), calls=%async_computation.4 | async-start | bytes 7962624
  82.1 3.1 copy-start
  137.6 0.6 copy-start.2
  157.3 0.7 copy-start.3
  157.3 0.7 copy-start.4
  157.3 259.9 %reduce-scatter.5.cloned.1.call-start = ((), (), s32[]{:S(2)}) async-start(), calls=%async_computation.3 | async-start | bytes 19464192 | tf_op jit(solution)/shard_map/reduce_scatter | solution.py:46
  169.5 1.1 copy-start.1
Sparse Core Ops, SparseCore 0:
  10.6 71.4 all-gather.1
  157.4 107.8 reduce-scatter.6
  268.6 148.5 reduce-scatter.4
where the time goes:
time: 424 us
  waiting for transfers between devices  240 us (57%)
  blocking collectives  119 us (28%)
  matrix products  31.3 us (7%)
  local copies, waits for them, and re-layouts  14 us (3%)
  between operations  13.8 us (3%)
  other arithmetic  6.05 us (1%)
    unnamed x4, waiting for transfers between devices  94.4 us
    all_gather x1, waiting for transfers between devices, shards(): gathered = lax.all_gather(hidden_input_state, 'tensor', axis=1, tiled=True)  74.1 us
    reduce_scatter x1, waiting for transfers between devices, shards(): lax.psum_scatter(lax.dot_general(normed, dlogits, (((0,), (0,)), ((), ())...  71 us
    psum x1, blocking collectives, shards(): lax.psum(jnp.sum(normed_gradient * normalized_slice, axis=0), 'dp')  54 us
    psum x1, blocking collectives, shards(): row_inner_sum = lax.psum(partial_inner_sum, 'tensor') / width  23.4 us
    pmax x1, blocking collectives, shards(): row_top = lax.pmax(local_top, 'tensor')  22.2 us
    psum x1, blocking collectives, shards(): row_total = lax.psum(local_total * jnp.exp(local_top - row_top), 'tensor')  19.1 us
    unnamed x14, local copies, waits for them, and re-layouts  13.2 us
  transfers between devices with their start and end apart: 3, of which 3 were waited for; matrix products, arithmetic and copies ran while one was open for 4% of the time, Pallas kernels for 0%

commit v1 on v0

--- a/solution.py
+++ b/solution.py
@@ -10,7 +10,10 @@
     local_cols = hidden_input_state.shape[1]
     vocab_rows = head_weight.shape[1]
     width = head_weight.shape[0]
-    gathered = lax.all_gather(hidden_input_state, "tensor", axis=1, tiled=True)
+    gathered = jnp.concatenate(
+        lax.all_to_all(jnp.stack([hidden_input_state] * lax.axis_size("tensor")), "tensor", 0, 0),
+        axis=1,
+    )
     values = gathered.astype(jnp.float32)
     scaled_rows = lax.rsqrt(jnp.mean(values * values, axis=1, keepdims=True) + epsilon)
     normed = (values * scaled_rows * norm_gain[None, :]).astype(jnp.bfloat16)

time: 424 us -> 403 us (0.950)
  waiting for transfers between devices: 240 us -> 208 us
  starting transfers between devices: 0.3 us -> 7.66 us
  matrix products: 31.3 us -> 26.7 us
    all_gather x1 -> x0, waiting for transfers between devices: 74.1 us -> none  [shards(): gathered = lax.all_gather(hidden_input_state, 'tensor', axis=1, tiled=True)]
    all_to_all x0 -> x1, waiting for transfers between devices: none -> 40.9 us  [shards(): lax.all_to_all(jnp.stack([hidden_input_state] * lax.axis_size('tensor')),...]
    all_to_all x0 -> x1, starting transfers between devices: none -> 7.43 us  [shards(): lax.all_to_all(jnp.stack([hidden_input_state] * lax.axis_size('tensor')),...]
    unnamed x4 -> x3, waiting for transfers between devices: 94.4 us -> 96.2 us
    unnamed x14 -> x12, local copies, waits for them, and re-layouts: 13.2 us -> 13.7 us
where the time goes in v1:
time: 403 us; the launch traced here: 402 us
  waiting for transfers between devices  208 us (52%)
  blocking collectives  119 us (30%)
  matrix products  26.7 us (7%)
  local copies, waits for them, and re-layouts  17.6 us (4%)
  between operations  14.1 us (3%)
  other arithmetic  8.52 us (2%)
  starting transfers between devices  7.66 us (2%)
    unnamed x3, waiting for transfers between devices  96.2 us
    reduce_scatter x1, waiting for transfers between devices, shards(): lax.psum_scatter(lax.dot_general(normed, dlogits, (((0,), (0,)), ((), ())...  71 us
    psum x1, blocking collectives, shards(): lax.psum(jnp.sum(normed_gradient * normalized_slice, axis=0), 'dp')  54 us
    all_to_all x1, waiting for transfers between devices, shards(): lax.all_to_all(jnp.stack([hidden_input_state] * lax.axis_size('tensor')),...  40.9 us
    psum x1, blocking collectives, shards(): row_inner_sum = lax.psum(partial_inner_sum, 'tensor') / width  23.4 us
    pmax x1, blocking collectives, shards(): row_top = lax.pmax(local_top, 'tensor')  22.3 us
    psum x1, blocking collectives, shards(): row_total = lax.psum(local_total * jnp.exp(local_top - row_top), 'tensor')  19.7 us
    unnamed x12, local copies, waits for them, and re-layouts  13.7 us
  transfers between devices with their start and end apart: 3, of which 3 were waited for; matrix products, arithmetic and copies ran while one was open for 4% of the time, Pallas kernels for 0%

profile of v1, /device:TPU:4, one launch (start us, length us, event | category | flops | bytes accessed | tf_op | source)
XLA Modules:
  0.0 402.1 jit_solution(9048101862160308798)
XLA Ops:
  7.2 3.1 stack.2
  10.2 7.4 %all-to-all-start = ((bf16[8,384,576]{1,2,0:T(8,128)(2,1)}), bf16[8,384,576]{1,2,0:T(8,128)(2,1)S(1)}, u32[]{:S(2)}, u32[]{:S(2)}) async-start(bf16[8,384,576]{1,2,0:T(8,128)(2,1)} %stack.2), calls=%async_computation | async-start | bytes 7077888 | tf_op jit(solution)/shard_map/all_to_all | solution.py:14
  17.7 0.0 reduce-scatter.7.cloned.1.call-start
  17.7 40.9 %all-to-all-done = bf16[8,384,576]{1,2,0:T(8,128)(2,1)S(1)} async-done(((bf16[8,384,576]{1,2,0:T(8,128)(2,1)}), bf16[8,384,576]{1,2,0:T(8,128)(2,1)S(1)}, u32[]{:S(2)}, u32[]{:S(2)}) %all-to-all-start) | async-done | bytes 3538976 | tf_op jit(solution)/shard_map/all_to_all | solution.py:14
  58.6 0.0 copy-start
  58.6 0.0 copy-start.1
  58.6 0.8 multiply_reduce_fusion
  59.4 1.0 copy-done
  60.4 3.9 fusion.1
  64.4 0.3 copy-done.1
  64.7 5.0 %fusion.4 = (f32[384]{0:T(512)S(1)}, f32[384,1024]{1,0:T(8,128)}) fusion(bf16[384,4608]{0,1:T(8,128)(2,1)S(1)} %fusion.1, bf16[4608,1024]{1,0:T(8,128)(2,1)S(1)} %copy-done.1), kind=kOutput, calls=%fused_computation.19 | convolution fusion | flops 3624271360 | bytes 14550528 | tf_op jit(solution)/shard_map/dot_general | solution.py:20
  69.7 22.3 %pmax.7 = f32[384]{0:T(512)S(1)} all-reduce(f32[384]{0:T(512)S(1)} %get-tuple-element.14), channel_id=1, replica_groups=mesh['dp'=32,'tensor'=8] {'tensor'}, use_global_device_ids=true, to_apply=%region_2.0 | all-reduce | flops 384 | bytes 3072 | tf_op jit(solution)/shard_map/pmax | solution.py:23
  92.0 1.8 exponential_reduce_fusion
  93.8 0.6 exponential_multiply_fusion
  94.4 19.7 %psum.21 = f32[384]{0:T(512)} all-reduce(f32[384]{0:T(512)} %exponential_multiply_fusion), channel_id=1, replica_groups=mesh['dp'=32,'tensor'=8] {'tensor'}, use_global_device_ids=true, to_apply=%region_4.0 | all-reduce | flops 384 | bytes 3072 | tf_op jit(solution)/shard_map/psum | solution.py:24
  114.0 0.7 log_add_fusion
  114.7 11.1 %convolution_bitcast_fusion = f32[4608,384]{0,1:T(8,128)} fusion(bf16[4608,1024]{1,0:T(8,128)(2,1)} %param.6, f32[384,1024]{1,0:T(8,128)} %get-tuple-element.15, s32[1024]{0:T(1024)S(1)} %iota_add_fusion, f32[384]{0:T(512)S(1)} %log_add_fusion, s32[384]{0:T(512)} %param.7), kind=kOutput, calls=%fused_computation | convolution fusion | flops 3625844736 | bytes 18095104 | tf_op jit(solution)/shard_map/dot_general | solution.py:34
  125.8 8.0 %copy.14 = f32[4608,384]{1,0:T(8,128)} copy(f32[4608,384]{0,1:T(8,128)} %convolution_bitcast_fusion) | data formatting | bytes 14155776
  133.8 0.0 copy-start.3
  133.8 0.0 reduce-scatter.7.cloned.1.call-update
  133.8 0.2 reduce-scatter.5.cloned.1.call-start
  134.1 0.4 copy-done.3
  134.5 10.7 %fusion.3 = f32[4608,1024]{1,0:T(8,128)} fusion(bf16[384,4608]{0,1:T(8,128)(2,1)S(1)} %fusion.1, f32[384,1024]{1,0:T(8,128)} %get-tuple-element.15, s32[1024]{0:T(1024)S(1)} %iota_add_fusion, f32[384]{0:T(512)S(1)} %log_add_fusion, s32[384]{0:T(512)S(1)} %copy-done.3), kind=kOutput, calls=%fused_computation.18 | convolution fusion | flops 3625844736 | bytes 23993344 | tf_op jit(solution)/shard_map/dot_general | solution.py:50
  145.2 0.0 copy-start.2
  145.2 0.0 reduce-scatter.5.cloned.1.call-update
  145.2 1.0 copy-done.2
  146.2 0.3 copy.12
  146.4 0.8 dynamic_slice.3
  147.2 96.1 %reduce-scatter.7.cloned.1.call-done = f32[576,384]{1,0:T(8,128)} async-done(((f32[4608,384]{1,0:T(8,128)}), f32[576,384]{1,0:T(8,128)}) %reduce-scatter.7.cloned.1.call-update) | async-done | bytes 884752
  243.4 1.5 copy.15
  244.9 0.4 fusion.2
  245.3 23.4 %psum.22 = f32[384]{0:T(512)S(1)} all-reduce(f32[384]{0:T(512)S(1)} %get-tuple-element.13), channel_id=1, replica_groups=mesh['dp'=32,'tensor'=8] {'tensor'}, use_global_device_ids=true, to_apply=%region_7.0 | all-reduce | flops 384 | bytes 3072 | tf_op jit(solution)/shard_map/psum | solution.py:43
  268.7 0.2 subtract_multiply_fusion
  269.0 1.2 copy.13
  270.2 54.0 %psum.23 = f32[576]{0:T(1024)} all-reduce(f32[576]{0:T(1024)S(1)} %get-tuple-element.12), channel_id=1, replica_groups=mesh['dp'=32,'tensor'=8] {'dp'}, use_global_device_ids=true, to_apply=%region_10.0 | all-reduce | flops 576 | bytes 4608 | tf_op jit(solution)/shard_map/psum | solution.py:48
  324.2 71.0 %reduce-scatter.5.cloned.1.call-done = f32[144,1024]{1,0:T(8,128)} async-done(((f32[4608,1024]{1,0:T(8,128)}), f32[144,1024]{1,0:T(8,128)}) %reduce-scatter.5.cloned.1.call-update) | async-done | bytes 589840 | tf_op jit(solution)/shard_map/reduce_scatter | solution.py:49
  (3 shorter events, 0.0 us)
Async XLA Ops:
  10.2 48.4 %all-to-all-start = ((bf16[8,384,576]{1,2,0:T(8,128)(2,1)}), bf16[8,384,576]{1,2,0:T(8,128)(2,1)S(1)}, u32[]{:S(2)}, u32[]{:S(2)}) async-start(bf16[8,384,576]{1,2,0:T(8,128)(2,1)} %stack.2), calls=%async_computation | async-start | bytes 7077888 | tf_op jit(solution)/shard_map/all_to_all | solution.py:14
  17.7 225.7 %reduce-scatter.7.cloned.1.call-start = ((), (), s32[]{:S(2)}) async-start(), calls=%async_computation.4 | async-start | bytes 7962624
  58.6 1.8 copy-start
  58.6 6.1 %copy-start.1 = (bf16[4608,1024]{1,0:T(8,128)(2,1)S(1)}, bf16[4608,1024]{1,0:T(8,128)(2,1)}, u32[]{:S(2)}) copy-start(bf16[4608,1024]{1,0:T(8,128)(2,1)} %param.6) | copy-start | bytes 28311556
  133.8 0.7 copy-start.3
  133.8 261.4 %reduce-scatter.5.cloned.1.call-start = ((), (), s32[]{:S(2)}) async-start(), calls=%async_computation.3 | async-start | bytes 19464192 | tf_op jit(solution)/shard_map/reduce_scatter | solution.py:49
  145.2 1.0 copy-start.2
Sparse Core Ops, SparseCore 0:
  134.0 109.3 reduce-scatter.6
  246.7 148.5 reduce-scatter.4
